TPU v7x, 512 devices: a whole 4x4x16 slice. The times are simulated.
512 devices in a mesh: expert: 32 (over y, z_hi, x), dp: 16 (over z_lo, core).
Axes of the slice: x: 4, y: 4, z: 16 (z_hi: 2, z_lo: 8; z = z_hi * 8 + z_lo), core: 2. Of those that a mesh axis runs over, the one named last changes fastest.
Arguments:
- tokens: bfloat16 [4096, 3584], P('expert'), may hold values from -6 to 6
- expert_ids: int32 [4096, 8], P('expert'), may hold values from 0 to 31, all different within a row; in each aligned block of 128 rows (0 to 127, 128 to 255, ...) at most 48 rows name the same one
- route_weights: float32 [4096, 8], P('expert'), may hold values from 0.05 to 0.45
- gate_up_panels: bfloat16 [32, 16, 1792, 256], P('expert', 'dp'), may hold values from -0.09375 to 0.09375
- down_panels: bfloat16 [32, 1024, 3584], P('expert', None, 'dp'), may hold values from -0.1875 to 0.1875
- partner: int32 [32], replicated, may hold values from 0 to 31, as said below
Outputs:
- moe_out: bfloat16 [4096, 3584], P('expert', 'dp')
- new_gate_up: bfloat16 [32, 16, 1792, 256], P('expert', 'dp')
- new_down: bfloat16 [32, 1024, 3584], P('expert', None, 'dp')
Inputs may be any that keep to these rules, and one draw needn't show every extreme that they name: `expert_ids`: in the 128 rows of one index of the expert axis, each row names 8 different experts and no expert is named by more than 48 rows. partner[i] is i, i XOR 1 or i XOR 2, the same of these for the four indices of each aligned group of four; partner[partner[i]] = i; some group takes XOR 1 and some group XOR 2.
All inputs are finite; a program needn't handle non-finite values.
Results may differ from a plain program's by a relative error of at most 0.0057.
Values may be sent and summed in bfloat16 or wider, within the bound.
No kernel may reach another device: no remote copies, remote signals or barrier semaphores. Data moves between devices by JAX's collectives and lax.ppermute only.
A program may use at most 64 MiB of HBM per device.

v0:
```python
import jax
import jax.numpy as jnp
from jax import lax
from jax.sharding import PartitionSpec as P


def from_partner(block, axis, bit):
    count = lax.axis_size(axis)
    route = []
    for low in range(count):
        high = low | 1 << bit
        if high != low and high < count:
            route += [(low, high), (high, low)]
    return lax.ppermute(block, axis, route)


def swap_panels(gate_up, down, partner):
    here = lax.axis_index("expert")
    partner_id = partner[here]
    result_gate_up, result_down = (gate_up, down)
    for bit_number in range(2):
        moved_gate_up, moved_down = from_partner((gate_up, down), "expert", bit_number)
        taken = partner_id == jnp.bitwise_xor(here, 1 << bit_number)
        result_gate_up = jnp.where(taken, moved_gate_up, result_gate_up)
        result_down = jnp.where(taken, moved_down, result_down)
    return (result_gate_up, result_down)


def run_layer(tokens, expert_ids, route_weights, gate_up, down, owner_table):
    devices = lax.axis_size("expert")
    token_rows, model_width = tokens.shape
    top_count = expert_ids.shape[1]
    expert_count = owner_table.shape[0]
    capacity = min(token_rows, 3 * token_rows * top_count // (2 * expert_count))
    half_width = model_width // 2
    side = lax.rem(lax.axis_index("dp"), 2)
    own_half = lax.dynamic_slice_in_dim(tokens, side * half_width, half_width, 1)
    labels = jnp.arange(expert_count, dtype=jnp.int32)
    onehot = (expert_ids[:, :, None] == labels[None, None, :]).astype(jnp.int32)
    picked = jnp.sum(onehot, axis=1)
    slot_rank = jnp.cumsum(picked, axis=0) - picked
    slots = jnp.sum(onehot * slot_rank[:, None, :], axis=2)
    target = jnp.sum(onehot * owner_table[None, None, :], axis=2)
    place = (target * capacity + slots).reshape(-1)
    row_ids = jnp.repeat(jnp.arange(token_rows, dtype=jnp.int32), top_count)
    source = jnp.full((devices * capacity,), token_rows, jnp.int32).at[place].set(row_ids)
    padded = jnp.concatenate([own_half, jnp.zeros((1, half_width), own_half.dtype)], axis=0)
    outgoing = padded[source].reshape(devices, capacity, half_width)
    arrived = lax.all_to_all(outgoing, "expert", split_axis=0, concat_axis=0, tiled=True)
    flat = arrived.reshape(devices * capacity, half_width)
    partial_value = jnp.dot(flat, gate_up, preferred_element_type=jnp.float32)
    half_rows = flat.shape[0] // 2
    mine = lax.dynamic_slice_in_dim(partial_value, side * half_rows, half_rows, 0)
    other = lax.dynamic_slice_in_dim(partial_value, (1 - side) * half_rows, half_rows, 0)
    summed = mine + from_partner(other, "dp", 0)
    block_units = gate_up.shape[1] // 2
    hidden = (jax.nn.silu(summed[:, :block_units]) * summed[:, block_units:]).astype(jnp.bfloat16)
    gathered = lax.all_gather(hidden, "dp", axis=1, tiled=True)
    pair_count = lax.axis_size("dp") // 2
    out_columns = down.shape[1]
    outputs = jnp.einsum(
        "rqhk,qkc->hrc",
        gathered.reshape(half_rows, pair_count, 2, block_units),
        down.reshape(pair_count, block_units, out_columns),
        preferred_element_type=jnp.float32,
    )
    expert_out = outputs.reshape(devices, capacity, out_columns).astype(jnp.bfloat16)
    returned = lax.all_to_all(expert_out, "expert", split_axis=0, concat_axis=0, tiled=True)
    chosen = returned.reshape(devices * capacity, out_columns)[place].reshape(
        token_rows, top_count, out_columns
    )
    mixed = jnp.sum(chosen.astype(jnp.float32) * route_weights[:, :, None], axis=1)
    return mixed.astype(jnp.bfloat16)


def per_device(tokens, expert_ids, route_weights, gate_up_panels, down_panels, partner):
    new_gate_up, new_down = swap_panels(gate_up_panels, down_panels, partner)
    moe_out = run_layer(tokens, expert_ids, route_weights, new_gate_up[0, 0], new_down[0], partner)
    return (moe_out, new_gate_up, new_down)


def solution(mesh):
    return jax.shard_map(
        per_device,
        mesh=mesh,
        in_specs=(
            P("expert", None),
            P("expert", None),
            P("expert", None),
            P("expert", "dp", None, None),
            P("expert", None, "dp"),
            P(),
        ),
        out_specs=(P("expert", "dp"), P("expert", "dp", None, None), P("expert", None, "dp")),
        check_vma=False,
    )
```

profile of v0, /device:TPU:1, one launch (start us, length us, event | category | flops | bytes accessed | tf_op | source)
XLA Modules:
  0.0 459.5 jit_solution(5787766010149977916)
XLA Ops:
  7.2 0.0 copy-start
  7.2 0.8 convert_reduce_fusion
  8.0 0.1 copy.24
  8.1 0.2 reduce_window_sum.11
  8.3 0.1 copy.26
  8.3 0.8 select_reduce_fusion.1
  9.1 0.1 copy.27
  9.2 0.1 add.55
  9.4 0.1 reshape.99
  9.5 4.3 scatter_custom_fusion
  13.8 0.0 copy-done
  13.9 6.7 %gather_fusion = bf16[1536,1792]{1,0:T(8,128)(2,1)} fusion(bf16[129,1792]{1,0:T(8,128)(2,1)S(1)} %concatenate.3, s32[2048]{0:T(1024)S(1)} %pad_clamp_fusion), kind=kCustom, calls=%fused_computation | custom fusion | bytes 11016192 | tf_op jit(solution)/shard_map/gather | solution.py:48
  20.7 0.0 copy-start.2
  20.7 0.0 copy-start.6
  20.7 21.4 %all-to-all-start = ((bf16[32,48,1792]{2,1,0:T(8,128)(2,1)}), bf16[32,48,1792]{2,1,0:T(8,128)(2,1)}, u32[]{:S(2)}, u32[]{:S(2)}) async-start(bf16[32,48,1792]{2,1,0:T(8,128)(2,1)} %bitcast.31), calls=%async_computation | async-start | bytes 11010048 | tf_op jit(solution)/shard_map/all_to_all | solution.py:49
  42.0 0.0 all-gather.2.cloned.1.call-start
  42.1 0.0 copy-done.2
  42.1 4.6 collective-permute-start.2
  46.7 2.2 collective-permute-start.3
  48.9 0.0 copy-done.6
  48.9 0.6 dynamic_slice.12
  50.8 80.2 %collective-permute-done.2 = bf16[1,1,1792,256]{3,2,1,0:T(8,128)(2,1)S(1)} collective-permute-done((bf16[1,1,1792,256]{3,2,1,0:T(8,128)(2,1)S(1)}, bf16[1,1,1792,256]{3,2,1,0:T(8,128)(2,1)S(1)}, u32[]{:S(2)}, u32[]{:S(2)}) %collective-permute-start.2) | collective-permute-done | bytes 917536 | tf_op jit(solution)/shard_map/ppermute | solution.py:14
  131.0 0.0 copy-start.4
  131.0 0.9 copy-done.4
  131.9 24.1 %collective-permute-done.3 = bf16[1,1,1792,256]{3,2,1,0:T(8,128)(2,1)} collective-permute-done((bf16[1,1,1792,256]{3,2,1,0:T(8,128)(2,1)S(1)}, bf16[1,1,1792,256]{3,2,1,0:T(8,128)(2,1)}, u32[]{:S(2)}, u32[]{:S(2)}) %collective-permute-start.3) | collective-permute-done | bytes 917536 | tf_op jit(solution)/shard_map/ppermute | solution.py:14
  156.0 1.3 select_select_fusion
  157.3 0.0 copy-start.3
  157.3 0.0 all-to-all-done
  157.3 4.5 fusion.12
  161.8 0.0 copy-done.3
  161.8 0.9 constant_dynamic-slice_fusion
  162.8 4.1 collective-permute-start.4
  166.9 2.1 collective-permute-done.4
  169.0 0.1 dynamic-slice_add_fusion
  169.1 0.8 fusion.16
  169.9 0.0 all-gather.2.cloned.1.call-update
  169.9 40.5 %collective-permute-start = (bf16[1,1024,224]{1,2,0:T(8,128)(2,1)}, bf16[1,1024,224]{1,2,0:T(8,128)(2,1)S(1)}, u32[]{:S(2)}, u32[]{:S(2)}) collective-permute-start(bf16[1,1024,224]{1,2,0:T(8,128)(2,1)} %param.10), channel_id=1, source_target_pairs={{0,32},{32,0},{16,48},{48,16},{64,96},{96,64},{80,112},{112,80},{1... | collective-permute-start | bytes 1376264 | tf_op jit(solution)/shard_map/ppermute | solution.py:14
  210.4 1.9 collective-permute-start.1
  212.3 8.8 %collective-permute-done = bf16[1,1024,224]{1,2,0:T(8,128)(2,1)S(1)} collective-permute-done((bf16[1,1024,224]{1,2,0:T(8,128)(2,1)}, bf16[1,1024,224]{1,2,0:T(8,128)(2,1)S(1)}, u32[]{:S(2)}, u32[]{:S(2)}) %collective-permute-start) | collective-permute-done | bytes 458784 | tf_op jit(solution)/shard_map/ppermute | solution.py:14
  221.1 8.9 %collective-permute-done.1 = bf16[1,1024,224]{1,2,0:T(8,128)(2,1)S(1)} collective-permute-done((bf16[1,1024,224]{1,2,0:T(8,128)(2,1)}, bf16[1,1024,224]{1,2,0:T(8,128)(2,1)S(1)}, u32[]{:S(2)}, u32[]{:S(2)}) %collective-permute-start.1) | collective-permute-done | bytes 458784 | tf_op jit(solution)/shard_map/ppermute | solution.py:14
  230.0 1.1 select_select_fusion.1
  231.1 0.0 copy-start.1
  231.1 0.1 copy.34
  231.2 157.7 %all-gather.2.cloned.1.call-done = bf16[768,2048]{1,0:T(8,128)(2,1)} async-done(((bf16[768,128]{1,0:T(8,128)(2,1)}), bf16[768,2048]{1,0:T(8,128)(2,1)}) %all-gather.2.cloned.1.call-update) | async-done | bytes 3145744 | tf_op jit(solution)/shard_map/all_gather | solution.py:58
  388.9 6.0 %reshape.76 = bf16[768,8,2,128]{3,2,1,0:T(2,128)(2,1)} reshape(bf16[768,2048]{1,0:T(8,128)(2,1)} %all-gather.2.cloned.1.call-done) | data formatting | bytes 6291456 | tf_op jit(solution)/shard_map/reshape | solution.py:63
  394.9 0.0 copy-done.1
  394.9 0.0 copy-start.5
  394.9 3.2 fusion.8
  398.1 1.2 copy.30
  399.3 10.9 %all-to-all-start.1 = ((bf16[32,48,224]{2,1,0:T(8,128)(2,1)}), bf16[32,48,224]{2,1,0:T(8,128)(2,1)S(1)}, u32[]{:S(2)}, u32[]{:S(2)}) async-start(bf16[32,48,224]{2,1,0:T(8,128)(2,1)} %bitcast.9), calls=%async_computation.1 | async-start | bytes 1572864 | tf_op jit(solution)/shard_map/all_to_all | solution.py:68
  410.2 0.0 copy-done.5
  410.2 0.1 copy.31
  410.3 37.3 %all-to-all-done.1 = bf16[32,48,224]{2,1,0:T(8,128)(2,1)S(1)} async-done(((bf16[32,48,224]{2,1,0:T(8,128)(2,1)}), bf16[32,48,224]{2,1,0:T(8,128)(2,1)S(1)}, u32[]{:S(2)}, u32[]{:S(2)}) %all-to-all-start.1) | async-done | bytes 688160 | tf_op jit(solution)/shard_map/all_to_all | solution.py:68
  447.6 3.9 gather_fusion.1
  451.6 0.4 fusion.11
  452.0 0.7 copy.32
  (9 shorter events, 0.1 us)
Async XLA Ops:
  7.2 6.7 %copy-start = (bf16[128,3584]{1,0:T(8,128)(2,1)S(1)}, bf16[128,3584]{1,0:T(8,128)(2,1)}, u32[]{:S(2)}) copy-start(bf16[128,3584]{1,0:T(8,128)(2,1)} %param.6) | copy-start | bytes 2752516
  20.7 21.4 %copy-start.2 = (bf16[1,1,1792,256]{3,2,1,0:T(8,128)(2,1)S(1)}, bf16[1,1,1792,256]{3,2,1,0:T(8,128)(2,1)}, u32[]{:S(2)}) copy-start(bf16[1,1,1792,256]{3,2,1,0:T(8,128)(2,1)} %param.9) | copy-start | bytes 2752516
  20.7 28.2 %copy-start.6 = (s32[32]{0:T(128)S(1)}, s32[32]{0:T(128)}, u32[]{:S(2)}) copy-start(s32[32]{0:T(128)} %param.11) | copy-start | bytes 388
  20.7 136.7 %all-to-all-start = ((bf16[32,48,1792]{2,1,0:T(8,128)(2,1)}), bf16[32,48,1792]{2,1,0:T(8,128)(2,1)}, u32[]{:S(2)}, u32[]{:S(2)}) async-start(bf16[32,48,1792]{2,1,0:T(8,128)(2,1)} %bitcast.31), calls=%async_computation | async-start | bytes 11010048 | tf_op jit(solution)/shard_map/all_to_all | solution.py:49
  42.0 346.9 %all-gather.2.cloned.1.call-start = ((), (), s32[]{:S(2)}) async-start(), calls=%async_computation.2 | async-start | bytes 3342336 | tf_op jit(solution)/shard_map/all_gather | solution.py:58
  42.1 88.9 %collective-permute-start.2 = (bf16[1,1,1792,256]{3,2,1,0:T(8,128)(2,1)S(1)}, bf16[1,1,1792,256]{3,2,1,0:T(8,128)(2,1)S(1)}, u32[]{:S(2)}, u32[]{:S(2)}) collective-permute-start(bf16[1,1,1792,256]{3,2,1,0:T(8,128)(2,1)S(1)} %copy-done.2), channel_id=1, source_target_pairs={{0,32},{32,0},{16,48},{48,16},{64,96},{96,64},{80,112},{112,80},{1... | collective-permute-start | bytes 2752520 | tf_op jit(solution)/shard_map/ppermute | solution.py:14
  46.7 109.3 %collective-permute-start.3 = (bf16[1,1,1792,256]{3,2,1,0:T(8,128)(2,1)S(1)}, bf16[1,1,1792,256]{3,2,1,0:T(8,128)(2,1)}, u32[]{:S(2)}, u32[]{:S(2)}) collective-permute-start(bf16[1,1,1792,256]{3,2,1,0:T(8,128)(2,1)S(1)} %copy-done.2), channel_id=1, source_target_pairs={{0,16},{16,0},{32,48},{48,32},{64,80},{80,64},{96,112},{112,96},{1... | collective-permute-start | bytes 2752520 | tf_op jit(solution)/shard_map/ppermute | solution.py:14
  131.0 0.9 copy-start.4
  157.3 4.5 copy-start.3
  162.8 6.2 %collective-permute-start.4 = (f32[768,256]{1,0:T(8,128)}, f32[768,256]{1,0:T(8,128)S(1)}, u32[]{:S(2)}, u32[]{:S(2)}) collective-permute-start(f32[768,256]{1,0:T(8,128)} %constant_dynamic-slice_fusion), channel_id=1, source_target_pairs={{0,1},{1,0},{2,3},{3,2},{4,5},{5,4},{6,7},{7,6},{8,9},{9,8},{10,11... | collective-permute-start | bytes 2359304 | tf_op jit(solution)/shard_map/ppermute | solution.py:14
  169.9 51.2 %collective-permute-start = (bf16[1,1024,224]{1,2,0:T(8,128)(2,1)}, bf16[1,1024,224]{1,2,0:T(8,128)(2,1)S(1)}, u32[]{:S(2)}, u32[]{:S(2)}) collective-permute-start(bf16[1,1024,224]{1,2,0:T(8,128)(2,1)} %param.10), channel_id=1, source_target_pairs={{0,32},{32,0},{16,48},{48,16},{64,96},{96,64},{80,112},{112,80},{1... | collective-permute-start | bytes 1376264 | tf_op jit(solution)/shard_map/ppermute | solution.py:14
  210.4 19.6 %collective-permute-start.1 = (bf16[1,1024,224]{1,2,0:T(8,128)(2,1)}, bf16[1,1024,224]{1,2,0:T(8,128)(2,1)S(1)}, u32[]{:S(2)}, u32[]{:S(2)}) collective-permute-start(bf16[1,1024,224]{1,2,0:T(8,128)(2,1)} %param.10), channel_id=1, source_target_pairs={{0,16},{16,0},{32,48},{48,32},{64,80},{80,64},{96,112},{112,96},{1... | collective-permute-start | bytes 1376264 | tf_op jit(solution)/shard_map/ppermute | solution.py:14
  231.1 163.8 %copy-start.1 = (bf16[1,1024,224]{1,2,0:T(8,128)(2,1)}, bf16[1,1024,224]{1,2,0:T(8,128)(2,1)S(1)}, u32[]{:S(2)}) copy-start(bf16[1,1024,224]{1,2,0:T(8,128)(2,1)S(1)} %select_select_fusion.1) | copy-start | bytes 1376260
  394.9 15.2 %copy-start.5 = (f32[128,8]{0,1:T(8,128)S(1)}, f32[128,8]{0,1:T(8,128)}, u32[]{:S(2)}) copy-start(f32[128,8]{0,1:T(8,128)} %param.8) | copy-start | bytes 12292
  399.3 48.3 %all-to-all-start.1 = ((bf16[32,48,224]{2,1,0:T(8,128)(2,1)}), bf16[32,48,224]{2,1,0:T(8,128)(2,1)S(1)}, u32[]{:S(2)}, u32[]{:S(2)}) async-start(bf16[32,48,224]{2,1,0:T(8,128)(2,1)} %bitcast.9), calls=%async_computation.1 | async-start | bytes 1572864 | tf_op jit(solution)/shard_map/all_to_all | solution.py:68
Sparse Core Ops, SparseCore 0:
  170.0 218.8 all-gather.1
where the time goes:
time: 460 us
  waiting for transfers between devices  319 us (69%)
  starting transfers between devices  85.5 us (19%)
  local copies, waits for them, and re-layouts  26.1 us (6%)
  between operations  15.6 us (3%)
  matrix products  7.64 us (2%)
  other arithmetic  5.51 us (1%)
    all_gather x1, waiting for transfers between devices, run_layer(): gathered = lax.all_gather(hidden, 'dp', axis=1, tiled=True)  158 us
    ppermute x5, waiting for transfers between devices, from_partner(): return lax.ppermute(block, axis, route)  124 us
    ppermute x5, starting transfers between devices, from_partner(): return lax.ppermute(block, axis, route)  53.3 us
    all_to_all x1, waiting for transfers between devices, run_layer(): lax.all_to_all(expert_out, 'expert', split_axis=0, concat_axis=0, tiled=T...  37.3 us
    all_to_all x1, starting transfers between devices, run_layer(): lax.all_to_all(outgoing, 'expert', split_axis=0, concat_axis=0, tiled=True)  21.4 us
    all_to_all x1, starting transfers between devices, run_layer(): lax.all_to_all(expert_out, 'expert', split_axis=0, concat_axis=0, tiled=T...  10.9 us
  transfers between devices with their start and end apart: 8, of which 7 were waited for; matrix products, arithmetic and copies ran while one was open for 1% of the time, Pallas kernels for 0%

commit v1 on v0

--- a/solution.py
+++ b/solution.py
@@ -55,7 +55,15 @@
     summed = mine + from_partner(other, "dp", 0)
     block_units = gate_up.shape[1] // 2
     hidden = (jax.nn.silu(summed[:, :block_units]) * summed[:, block_units:]).astype(jnp.bfloat16)
-    gathered = lax.all_gather(hidden, "dp", axis=1, tiled=True)
+
+    def _tell_local_data(x_in, axis_key):
+        now = lax.axis_size(axis_key)
+        lower = jnp.stack(now * [x_in], axis=0)
+        value_now = lax.all_to_all(lower, axis_key, 0, 0)
+        heard = jnp.concatenate(value_now, axis=1)
+        return heard
+
+    gathered = _tell_local_data(hidden, "dp")
     pair_count = lax.axis_size("dp") // 2
     out_columns = down.shape[1]
     outputs = jnp.einsum(

time: 460 us -> 500 us (1.087)
  the two profiles are of different devices: /device:TPU:1 before, /device:TPU:482 now
where the time goes in v1:
time: 500 us; the launch traced here: 499 us
  waiting for transfers between devices  265 us (53%)
  starting transfers between devices  199 us (40%)
  local copies, waits for them, and re-layouts  22.4 us (4%)
  matrix products  7.49 us (1%)
    all_to_all x1, starting transfers between devices, _tell_local_data(): value_now = lax.all_to_all(lower, axis_key, 0, 0)  143 us
    ppermute x5, waiting for transfers between devices, from_partner(): return lax.ppermute(block, axis, route)  123 us
    all_to_all x1, waiting for transfers between devices, _tell_local_data(): value_now = lax.all_to_all(lower, axis_key, 0, 0)  109 us
    all_to_all x1, waiting for transfers between devices, run_layer(): lax.all_to_all(expert_out, 'expert', split_axis=0, concat_axis=0, tiled=T...  33.2 us
    all_to_all x1, starting transfers between devices, run_layer(): lax.all_to_all(expert_out, 'expert', split_axis=0, concat_axis=0, tiled=T...  23.4 us
    all_to_all x1, starting transfers between devices, run_layer(): lax.all_to_all(outgoing, 'expert', split_axis=0, concat_axis=0, tiled=True)  17.4 us
    ppermute x5, starting transfers between devices, from_partner(): return lax.ppermute(block, axis, route)  14.6 us
  transfers between devices with their start and end apart: 8, of which 7 were waited for; matrix products, arithmetic and copies ran while one was open for 0% of the time, Pallas kernels for 0%

profile of v1, /device:TPU:482, one launch (start us, length us, event | category | flops | bytes accessed | tf_op | source)
XLA Modules:
  0.0 499.1 jit_solution(1747829135669584273)
XLA Ops:
  0.6 0.0 copy-start
  0.7 0.8 convert_reduce_fusion
  1.4 0.1 copy.23
  1.5 0.2 reduce_window_sum.11
  1.7 0.1 copy.25
  1.8 0.8 select_reduce_fusion.1
  2.6 0.1 copy.26
  2.7 0.1 add.55
  2.8 0.1 reshape.101
  2.9 4.3 scatter_custom_fusion
  7.3 0.0 copy-done
  7.4 6.7 %gather_fusion = bf16[1536,1792]{1,0:T(8,128)(2,1)} fusion(bf16[129,1792]{1,0:T(8,128)(2,1)S(1)} %concatenate.3, s32[2048]{0:T(1024)S(1)} %pad_clamp_fusion), kind=kCustom, calls=%fused_computation | custom fusion | bytes 11016192 | tf_op jit(solution)/shard_map/gather | solution.py:48
  14.1 0.0 copy-start.2
  14.1 0.0 copy-start.7
  14.1 17.4 %all-to-all-start = ((bf16[32,48,1792]{2,1,0:T(8,128)(2,1)}), bf16[32,48,1792]{2,1,0:T(8,128)(2,1)}, u32[]{:S(2)}, u32[]{:S(2)}) async-start(bf16[32,48,1792]{2,1,0:T(8,128)(2,1)} %bitcast.39), calls=%async_computation | async-start | bytes 11010048 | tf_op jit(solution)/shard_map/all_to_all | solution.py:49
  31.6 0.0 copy-done.2
  31.6 4.0 collective-permute-start.2
  35.5 3.4 collective-permute-start.3
  38.9 0.0 copy-done.7
  38.9 0.6 dynamic_slice.12
  40.8 83.4 %collective-permute-done.2 = bf16[1,1,1792,256]{3,2,1,0:T(8,128)(2,1)S(1)} collective-permute-done((bf16[1,1,1792,256]{3,2,1,0:T(8,128)(2,1)S(1)}, bf16[1,1,1792,256]{3,2,1,0:T(8,128)(2,1)S(1)}, u32[]{:S(2)}, u32[]{:S(2)}) %collective-permute-start.2) | collective-permute-done | bytes 917536 | tf_op jit(solution)/shard_map/ppermute | solution.py:14
  124.3 0.0 copy-start.4
  124.3 0.9 copy-done.4
  125.2 18.6 %collective-permute-done.3 = bf16[1,1,1792,256]{3,2,1,0:T(8,128)(2,1)} collective-permute-done((bf16[1,1,1792,256]{3,2,1,0:T(8,128)(2,1)S(1)}, bf16[1,1,1792,256]{3,2,1,0:T(8,128)(2,1)}, u32[]{:S(2)}, u32[]{:S(2)}) %collective-permute-start.3) | collective-permute-done | bytes 917536 | tf_op jit(solution)/shard_map/ppermute | solution.py:14
  143.8 1.3 select_select_fusion
  145.1 0.0 copy-start.3
  145.1 0.0 all-to-all-done
  145.1 4.5 fusion.3
  149.6 0.0 copy-done.3
  149.6 0.9 constant_dynamic-slice_fusion
  150.5 1.9 collective-permute-start.4
  152.5 2.5 collective-permute-done.4
  154.9 0.1 dynamic-slice_add_fusion
  155.0 0.1 fusion.7
  155.2 2.3 stack.2
  157.4 0.0 copy-start.5
  157.4 143.2 %all-to-all-start.1 = ((bf16[16,768,128]{2,1,0:T(8,128)(2,1)}), bf16[16,768,128]{2,1,0:T(8,128)(2,1)}, u32[]{:S(2)}, u32[]{:S(2)}) async-start(bf16[16,768,128]{2,1,0:T(8,128)(2,1)} %stack.2), calls=%async_computation.1 | async-start | bytes 6291456 | tf_op jit(solution)/shard_map/all_to_all | solution.py:62
  300.6 0.0 copy-done.5
  300.6 1.9 collective-permute-start
  302.5 3.4 collective-permute-start.1
  306.0 11.4 %collective-permute-done = bf16[1,1024,224]{1,2,0:T(8,128)(2,1)S(1)} collective-permute-done((bf16[1,1024,224]{1,2,0:T(8,128)(2,1)S(1)}, bf16[1,1024,224]{1,2,0:T(8,128)(2,1)S(1)}, u32[]{:S(2)}, u32[]{:S(2)}) %collective-permute-start) | collective-permute-done | bytes 458784 | tf_op jit(solution)/shard_map/ppermute | solution.py:14
  317.4 7.0 %collective-permute-done.1 = bf16[1,1024,224]{1,2,0:T(8,128)(2,1)S(1)} collective-permute-done((bf16[1,1024,224]{1,2,0:T(8,128)(2,1)S(1)}, bf16[1,1024,224]{1,2,0:T(8,128)(2,1)S(1)}, u32[]{:S(2)}, u32[]{:S(2)}) %collective-permute-start.1) | collective-permute-done | bytes 458784 | tf_op jit(solution)/shard_map/ppermute | solution.py:14
  324.4 0.1 select_select_fusion.1
  324.4 0.0 copy-start.1
  324.4 0.1 copy.33
  324.5 108.6 %all-to-all-done.1 = bf16[16,768,128]{2,1,0:T(8,128)(2,1)} async-done(((bf16[16,768,128]{2,1,0:T(8,128)(2,1)}), bf16[16,768,128]{2,1,0:T(8,128)(2,1)}, u32[]{:S(2)}, u32[]{:S(2)}) %all-to-all-start.1) | async-done | bytes 3145760 | tf_op jit(solution)/shard_map/all_to_all | solution.py:62
  433.1 0.0 copy-start.6
  433.1 3.0 fusion.1
  436.1 1.2 copy.29
  437.3 0.0 copy-done.1
  437.3 23.4 %all-to-all-start.2 = ((bf16[32,48,224]{2,1,0:T(8,128)(2,1)}), bf16[32,48,224]{2,1,0:T(8,128)(2,1)S(1)}, u32[]{:S(2)}, u32[]{:S(2)}) async-start(bf16[32,48,224]{2,1,0:T(8,128)(2,1)} %bitcast.11), calls=%async_computation.2 | async-start | bytes 1572864 | tf_op jit(solution)/shard_map/all_to_all | solution.py:76
  460.7 0.0 copy-done.6
  460.7 0.1 copy.30
  460.8 33.2 %all-to-all-done.2 = bf16[32,48,224]{2,1,0:T(8,128)(2,1)S(1)} async-done(((bf16[32,48,224]{2,1,0:T(8,128)(2,1)}), bf16[32,48,224]{2,1,0:T(8,128)(2,1)S(1)}, u32[]{:S(2)}, u32[]{:S(2)}) %all-to-all-start.2) | async-done | bytes 688160 | tf_op jit(solution)/shard_map/all_to_all | solution.py:76
  494.0 3.9 gather_fusion.1
  497.9 0.4 fusion.2
  498.3 0.7 copy.31
  (9 shorter events, 0.1 us)
Async XLA Ops:
  0.6 6.7 %copy-start = (bf16[128,3584]{1,0:T(8,128)(2,1)S(1)}, bf16[128,3584]{1,0:T(8,128)(2,1)}, u32[]{:S(2)}) copy-start(bf16[128,3584]{1,0:T(8,128)(2,1)} %param.6) | copy-start | bytes 2752516
  14.1 17.4 %copy-start.2 = (bf16[1,1,1792,256]{3,2,1,0:T(8,128)(2,1)S(1)}, bf16[1,1,1792,256]{3,2,1,0:T(8,128)(2,1)}, u32[]{:S(2)}) copy-start(bf16[1,1,1792,256]{3,2,1,0:T(8,128)(2,1)} %param.9) | copy-start | bytes 2752516
  14.1 24.8 %copy-start.7 = (s32[32]{0:T(128)S(1)}, s32[32]{0:T(128)}, u32[]{:S(2)}) copy-start(s32[32]{0:T(128)} %param.11) | copy-start | bytes 388
  14.1 130.9 %all-to-all-start = ((bf16[32,48,1792]{2,1,0:T(8,128)(2,1)}), bf16[32,48,1792]{2,1,0:T(8,128)(2,1)}, u32[]{:S(2)}, u32[]{:S(2)}) async-start(bf16[32,48,1792]{2,1,0:T(8,128)(2,1)} %bitcast.39), calls=%async_computation | async-start | bytes 11010048 | tf_op jit(solution)/shard_map/all_to_all | solution.py:49
  31.6 92.7 %collective-permute-start.2 = (bf16[1,1,1792,256]{3,2,1,0:T(8,128)(2,1)S(1)}, bf16[1,1,1792,256]{3,2,1,0:T(8,128)(2,1)S(1)}, u32[]{:S(2)}, u32[]{:S(2)}) collective-permute-start(bf16[1,1,1792,256]{3,2,1,0:T(8,128)(2,1)S(1)} %copy-done.2), channel_id=1, source_target_pairs={{0,32},{32,0},{16,48},{48,16},{64,96},{96,64},{80,112},{112,80},{1... | collective-permute-start | bytes 2752520 | tf_op jit(solution)/shard_map/ppermute | solution.py:14
  35.5 108.2 %collective-permute-start.3 = (bf16[1,1,1792,256]{3,2,1,0:T(8,128)(2,1)S(1)}, bf16[1,1,1792,256]{3,2,1,0:T(8,128)(2,1)}, u32[]{:S(2)}, u32[]{:S(2)}) collective-permute-start(bf16[1,1,1792,256]{3,2,1,0:T(8,128)(2,1)S(1)} %copy-done.2), channel_id=1, source_target_pairs={{0,16},{16,0},{32,48},{48,32},{64,80},{80,64},{96,112},{112,96},{1... | collective-permute-start | bytes 2752520 | tf_op jit(solution)/shard_map/ppermute | solution.py:14
  124.3 0.9 copy-start.4
  145.1 4.5 copy-start.3
  150.5 4.4 collective-permute-start.4
  157.4 143.2 %copy-start.5 = (bf16[1,1024,224]{1,2,0:T(8,128)(2,1)S(1)}, bf16[1,1024,224]{1,2,0:T(8,128)(2,1)}, u32[]{:S(2)}) copy-start(bf16[1,1024,224]{1,2,0:T(8,128)(2,1)} %param.10) | copy-start | bytes 1376260
  157.4 275.7 %all-to-all-start.1 = ((bf16[16,768,128]{2,1,0:T(8,128)(2,1)}), bf16[16,768,128]{2,1,0:T(8,128)(2,1)}, u32[]{:S(2)}, u32[]{:S(2)}) async-start(bf16[16,768,128]{2,1,0:T(8,128)(2,1)} %stack.2), calls=%async_computation.1 | async-start | bytes 6291456 | tf_op jit(solution)/shard_map/all_to_all | solution.py:62
  300.6 16.8 %collective-permute-start = (bf16[1,1024,224]{1,2,0:T(8,128)(2,1)S(1)}, bf16[1,1024,224]{1,2,0:T(8,128)(2,1)S(1)}, u32[]{:S(2)}, u32[]{:S(2)}) collective-permute-start(bf16[1,1024,224]{1,2,0:T(8,128)(2,1)S(1)} %copy-done.5), channel_id=1, source_target_pairs={{0,32},{32,0},{16,48},{48,16},{64,96},{96,64},{80,112},{112,80},{1... | collective-permute-start | bytes 1376264 | tf_op jit(solution)/shard_map/ppermute | solution.py:14
  302.5 21.8 %collective-permute-start.1 = (bf16[1,1024,224]{1,2,0:T(8,128)(2,1)S(1)}, bf16[1,1024,224]{1,2,0:T(8,128)(2,1)S(1)}, u32[]{:S(2)}, u32[]{:S(2)}) collective-permute-start(bf16[1,1024,224]{1,2,0:T(8,128)(2,1)S(1)} %copy-done.5), channel_id=1, source_target_pairs={{0,16},{16,0},{32,48},{48,32},{64,80},{80,64},{96,112},{112,96},{1... | collective-permute-start | bytes 1376264 | tf_op jit(solution)/shard_map/ppermute | solution.py:14
  324.4 112.8 %copy-start.1 = (bf16[1,1024,224]{1,2,0:T(8,128)(2,1)}, bf16[1,1024,224]{1,2,0:T(8,128)(2,1)S(1)}, u32[]{:S(2)}) copy-start(bf16[1,1024,224]{1,2,0:T(8,128)(2,1)S(1)} %select_select_fusion.1) | copy-start | bytes 1376260
  433.1 27.6 %copy-start.6 = (f32[128,8]{0,1:T(8,128)S(1)}, f32[128,8]{0,1:T(8,128)}, u32[]{:S(2)}) copy-start(f32[128,8]{0,1:T(8,128)} %param.8) | copy-start | bytes 12292
  437.3 56.7 %all-to-all-start.2 = ((bf16[32,48,224]{2,1,0:T(8,128)(2,1)}), bf16[32,48,224]{2,1,0:T(8,128)(2,1)S(1)}, u32[]{:S(2)}, u32[]{:S(2)}) async-start(bf16[32,48,224]{2,1,0:T(8,128)(2,1)} %bitcast.11), calls=%async_computation.2 | async-start | bytes 1572864 | tf_op jit(solution)/shard_map/all_to_all | solution.py:76
